TPU v7x, 128 devices: a whole 4x4x4 slice. The times are simulated.
128 devices in a mesh: fsdp: 8 (over x, z_lo), dp: 16 (over z_hi, y, core).
Axes of the slice: x: 4, y: 4, z: 4 (z_hi: 2, z_lo: 2; z = z_hi * 2 + z_lo), core: 2. Of those that a mesh axis runs over, the one named last changes fastest.
Arguments:
- tokens: bfloat16 [8, 2176, 3200], P('fsdp', 'dp'), may hold values from -6 to 6
- norm_gain: float32 [3200], replicated, may hold values from 0.5 to 1.5
- qkv_weight: bfloat16 [3200, 6144], P('fsdp', 'dp'), may hold values from -4 to 4
- qk_gain: float32 [2, 2048], P(None, 'dp'), may hold values from 1 to 8
- out_weight: bfloat16 [2048, 3200], P('dp', 'fsdp'), may hold values from -0.125 to 0.125
- layer_scale: float32 [3200], replicated, may hold values from 0.2 to 1
- tile_counts: int32 [8, 2], replicated, may hold values from 0 to 2, as said below
- owners: int32 [8, 2], replicated, may hold values from 0 to 7, as said below
Outputs:
- vision_tokens: bfloat16 [32, 256, 12800], P('fsdp', None, 'dp')
Inputs may be any that keep to these rules, and one draw needn't show every extreme that they name: `tile_counts`: column 0 is 1 to 2, column 1 is 0 to 2 minus column 0. All owners together get at most 4 live tiles each, and one owner gets exactly 4.
All inputs are finite; a program needn't handle non-finite values.
Results may differ from a plain program's by a relative error of at most 0.006.
The roundings to bfloat16 on the way count: a program that leaves them out, or rounds other values in their place, can miss the bound.
Values may be sent and summed in bfloat16 or wider, within the bound.
No kernel may reach another device: no remote copies, remote signals or barrier semaphores. Data moves between devices by JAX's collectives and lax.ppermute only.
A program may use at most 192 MiB of HBM per device.

v0:
```python
import jax
import jax.numpy as jnp
from jax import lax
from jax.sharding import Mesh, PartitionSpec as P

HEAD_DIM = 128
GRID = 32
SLOTS = 2
TILE = 1025
CAP = 4
EPSILON = 1e-06


def merge_tiles(values):
    halves = GRID // 2
    columns = values.shape[1]
    tile_list = []
    for tile_slot in range(SLOTS):
        patches = values[tile_slot * TILE + 1 : (tile_slot + 1) * TILE]
        square = patches.reshape(halves, 2, halves, 2, columns).transpose(0, 2, 4, 1, 3)
        tile_list.append(square.reshape(halves * halves, columns * 4))
    return jnp.stack(tile_list)


def tile_owners(tile_counts, owners):
    slot_index = jnp.arange(SLOTS, dtype=jnp.int32)[None, :]
    first_count = tile_counts[:, 0:1]
    holder = jnp.where(slot_index < first_count, owners[:, 0:1], owners[:, 1:2])
    living = slot_index < first_count + tile_counts[:, 1:2]
    return (holder, living)


def place_tiles(received, holder, living, target):
    owned_flag = jnp.logical_and(living, holder == target).reshape(-1).astype(jnp.int32)
    before = jnp.cumsum(owned_flag) - owned_flag
    flattened = received.reshape((received.shape[0] * received.shape[1],) + received.shape[2:])
    sources = jnp.arange(flattened.shape[0], dtype=jnp.int32)
    placed = []
    for slot in range(CAP):
        match = jnp.logical_and(before == slot, owned_flag == 1)
        source = jnp.max(jnp.where(match, sources, 0))
        tile = lax.dynamic_index_in_dim(flattened, source, axis=0, keepdims=False)
        placed.append(jnp.where(jnp.any(match), tile, jnp.zeros((), tile.dtype)))
    return jnp.stack(placed)


def gather_sum(values, axis_name, groups):
    spread = jnp.broadcast_to(values[None], (groups,) + values.shape)
    collected = lax.all_to_all(spread, axis_name, split_axis=0, concat_axis=0, tiled=True)
    return jnp.sum(collected, axis=0)


def gather_blocks(block_value, axis_name, groups):
    spread = jnp.broadcast_to(block_value[None], (groups,) + block_value.shape)
    collected = lax.all_to_all(spread, axis_name, split_axis=0, concat_axis=0, tiled=True)
    return collected.reshape((groups * block_value.shape[0],) + block_value.shape[1:])


def pair_up(value, core, swap, axis):
    other = lax.ppermute(value, "core", swap)
    low = jnp.where(core == 0, value, other)
    high = jnp.where(core == 0, other, value)
    return jnp.concatenate([low, high], axis=axis)


def body(tokens, norm_gain, qkv_weight, qk_gain, out_weight, layer_scale, tile_counts, owners):
    own_rows = tokens[0]
    chips = lax.axis_size("chip")
    cores = lax.axis_size("core")
    groups = chips * cores
    chip = lax.axis_index("chip")
    core = lax.axis_index("core")
    row_index = lax.axis_index("fsdp")
    row_count = lax.axis_size("fsdp")
    model_width = own_rows.shape[1]
    block = model_width // groups
    swap = [(0, 1), (1, 0)]
    spread = jnp.broadcast_to(out_weight[None], (row_count,) + out_weight.shape)
    head_rows = lax.all_to_all(spread, "fsdp", split_axis=0, concat_axis=0, tiled=True)
    per_row = out_weight.shape[1] // block
    head_rows = head_rows.reshape(row_count, HEAD_DIM, per_row, block).transpose(0, 2, 1, 3)
    weight_block = lax.all_to_all(
        head_rows.reshape(groups, HEAD_DIM, block),
        ("chip", "core"),
        split_axis=0,
        concat_axis=0,
        tiled=True,
    ).reshape(groups * HEAD_DIM, block)
    pair_weight = pair_up(weight_block, core, swap, 1)
    full_qkv = gather_blocks(qkv_weight, "fsdp", row_count)
    pair_qkv = pair_up(full_qkv, core, swap, 1)
    pair_qkv, pair_weight = lax.optimization_barrier((pair_qkv, pair_weight))
    pair_gain = pair_up(qk_gain, core, swap, 1).reshape(2, cores, HEAD_DIM)
    half = lax.all_gather(own_rows, "chip", axis=0, tiled=True)
    half_length = half.shape[0]
    piece = own_rows.shape[0]
    values = half.astype(jnp.float32)
    normed = (
        values * lax.rsqrt(jnp.mean(values * values, axis=-1, keepdims=True) + EPSILON) * norm_gain
    ).astype(jnp.bfloat16)
    projected = jnp.dot(normed, pair_qkv, preferred_element_type=jnp.float32)
    projected = projected.reshape(half_length, cores, 3, HEAD_DIM)
    queries = projected[:, :, 0]
    keys_part = projected[:, :, 1]
    values_part = projected[:, :, 2].astype(jnp.bfloat16)
    sums = gather_sum(
        jnp.stack(
            [jnp.sum(queries * queries, axis=(1, 2)), jnp.sum(keys_part * keys_part, axis=(1, 2))]
        ),
        "chip",
        chips,
    )
    window = groups * HEAD_DIM
    queries = (
        queries * lax.rsqrt(sums[0] / window + EPSILON)[:, None, None] * pair_gain[0][None]
    ).astype(jnp.bfloat16)
    keys_part = (
        keys_part * lax.rsqrt(sums[1] / window + EPSILON)[:, None, None] * pair_gain[1][None]
    ).astype(jnp.bfloat16)
    stacked = jnp.stack([queries, keys_part, values_part])
    mine = lax.dynamic_index_in_dim(stacked, core, axis=2, keepdims=False)
    theirs = lax.dynamic_index_in_dim(stacked, 1 - core, axis=2, keepdims=False)
    got = lax.ppermute(theirs, "core", swap)
    first_half = jnp.where(core == 0, mine, got).reshape(3, chips, piece, HEAD_DIM)
    second_half = jnp.where(core == 0, got, mine).reshape(3, chips, piece, HEAD_DIM)
    whole = jnp.stack([first_half, second_half], axis=2).reshape(3, groups * piece, HEAD_DIM)
    length = whole.shape[1]
    factor = HEAD_DIM ** (-0.5)
    covered = SLOTS * TILE
    tile_query = whole[0, :covered].reshape(SLOTS, TILE, HEAD_DIM)
    tile_key = whole[1, :covered].reshape(SLOTS, TILE, HEAD_DIM)
    tile_value = whole[2, :covered].reshape(SLOTS, TILE, HEAD_DIM)
    scores = (
        jnp.einsum("sqc,skc->sqk", tile_query, tile_key, preferred_element_type=jnp.float32)
        * factor
    )
    highest = jnp.max(scores, axis=-1, keepdims=True)
    exponent = jnp.exp(scores - highest)
    weights = (exponent / jnp.sum(exponent, axis=-1, keepdims=True)).astype(jnp.bfloat16)
    tile_out = jnp.einsum(
        "sqk,skc->sqc", weights, tile_value, preferred_element_type=jnp.float32
    ).astype(jnp.bfloat16)
    head_out = jnp.concatenate(
        [
            tile_out.reshape(covered, HEAD_DIM),
            jnp.zeros((length - covered, HEAD_DIM), jnp.bfloat16),
        ],
        axis=0,
    )
    by_half = head_out.reshape(chips, cores, piece, HEAD_DIM).transpose(1, 0, 2, 3)
    by_half = by_half.reshape(cores, half_length, HEAD_DIM)
    outgoing = jnp.broadcast_to(by_half[None], (chips, cores, half_length, HEAD_DIM))
    all_heads = lax.all_to_all(
        outgoing.reshape(groups, half_length, HEAD_DIM),
        ("chip", "core"),
        split_axis=0,
        concat_axis=0,
        tiled=True,
    )
    head_terms = jnp.einsum(
        "hsc,hcd->hsd",
        all_heads,
        pair_weight.reshape(groups, HEAD_DIM, cores * block),
        preferred_element_type=jnp.float32,
    ).astype(jnp.bfloat16)
    attention = jnp.sum(lax.optimization_barrier(head_terms).astype(jnp.float32), axis=0)
    pair_tokens = lax.dynamic_slice_in_dim(half, chip * cores * block, cores * block, axis=1)
    pair_scale = lax.dynamic_slice_in_dim(layer_scale, chip * cores * block, cores * block)
    updated_half = (pair_tokens.astype(jnp.float32) + pair_scale * attention).astype(jnp.bfloat16)
    keep = lax.dynamic_slice_in_dim(updated_half, core * block, block, axis=1)
    give = lax.dynamic_slice_in_dim(updated_half, (1 - core) * block, block, axis=1)
    taken = lax.ppermute(give, "core", swap)
    first_half = jnp.where(core == 0, keep, taken).reshape(chips, piece, block)
    second_half = jnp.where(core == 0, taken, keep).reshape(chips, piece, block)
    updated = jnp.stack([first_half, second_half], axis=1).reshape(length, block)
    merged = merge_tiles(updated)
    holder, living = tile_owners(tile_counts, owners)
    own_holder = holder[row_index]
    own_living = living[row_index]
    destination = jnp.arange(row_count, dtype=jnp.int32)[:, None]
    sending = jnp.logical_and(destination == own_holder[None, :], own_living[None, :])
    outgoing = jnp.where(sending[:, :, None, None], merged[None], jnp.zeros((), jnp.bfloat16))
    received = lax.all_to_all(outgoing, "fsdp", split_axis=0, concat_axis=0, tiled=True)
    return place_tiles(received, holder, living, row_index)


def solution(mesh):
    fsdp_size = mesh.shape["fsdp"]
    dp_size = mesh.shape["dp"]
    split = Mesh(mesh.devices.reshape(fsdp_size, dp_size // 2, 2), ("fsdp", "chip", "core"))
    heads = ("chip", "core")
    placed = (
        P("fsdp", heads, None),
        P(),
        P("fsdp", heads),
        P(None, heads),
        P(heads, "fsdp"),
        P(),
        P(),
        P(),
    )
    return jax.shard_map(
        body, mesh=split, in_specs=placed, out_specs=P("fsdp", None, heads), check_vma=False
    )
```

profile of v0, /device:TPU:8, one launch (start us, length us, event | category | flops | bytes accessed | tf_op | source)
XLA Modules:
  0.0 395.8 jit_solution(15600557721737662386)
XLA Ops:
  6.5 0.7 all-gather.3.cloned.1.call-update
  7.3 1.0 broadcast_in_dim.95
  8.3 19.0 %all_to_all.30 = bf16[8,128,400]{1,2,0:T(8,128)(2,1)S(1)} all-to-all(bf16[8,128,400]{1,2,0:T(8,128)(2,1)S(1)} %broadcast_in_dim.95), channel_id=1, replica_groups=mesh['fsdp'=8,'chip'=8,'core'=2] {'fsdp'}, dimensions={0} | all-to-all | bytes 1638400 | tf_op jit(solution)/shard_map/all_to_all | solution.py:79
  27.3 1.7 broadcast_in_dim.94
  29.0 3.6 all-to-all-start
  32.9 1.2 reshape.266
  34.1 2.3 copy.108
  36.4 30.7 %all-to-all-done = bf16[8,400,384]{2,1,0:T(8,128)(2,1)S(1)} async-done(((bf16[8,400,384]{2,1,0:T(8,128)(2,1)}), bf16[8,400,384]{2,1,0:T(8,128)(2,1)S(1)}, u32[]{:S(2)}, u32[]{:S(2)}) %all-to-all-start) | async-done | bytes 2457632 | tf_op jit(solution)/shard_map/all_to_all | solution.py:55
  67.1 8.0 %all-to-all-start.2 = ((bf16[16,128,200]{1,2,0:T(8,128)(2,1)}), bf16[16,128,200]{1,2,0:T(8,128)(2,1)S(1)}, u32[]{:S(2)}, u32[]{:S(2)}) async-start(bf16[16,128,200]{1,2,0:T(8,128)(2,1)} %copy.108), calls=%async_computation.2 | async-start | bytes 1638400 | tf_op jit(solution)/shard_map/all_to_all | solution.py:82
  75.2 15.0 %all-to-all-done.2 = bf16[16,128,200]{1,2,0:T(8,128)(2,1)S(1)} async-done(((bf16[16,128,200]{1,2,0:T(8,128)(2,1)}), bf16[16,128,200]{1,2,0:T(8,128)(2,1)S(1)}, u32[]{:S(2)}, u32[]{:S(2)}) %all-to-all-start.2) | async-done | bytes 819232 | tf_op jit(solution)/shard_map/all_to_all | solution.py:82
  90.1 1.0 copy_bitcast_fusion
  91.1 0.7 collective-permute-start.1
  91.8 2.3 collective-permute-done.2
  94.1 0.5 fusion.31
  94.6 1.5 broadcast_select_fusion.4
  96.1 1.3 pad_maximum_fusion.3
  97.4 2.1 broadcast_select_fusion.2
  99.6 2.7 pad_maximum_fusion
  102.2 26.1 %all-gather.3.cloned.1.call-done = bf16[1,1088,3200]{2,1,0:T(8,128)(2,1)} async-done(((bf16[1,136,3200]{2,1,0:T(8,128)(2,1)}), bf16[1,1088,3200]{2,1,0:T(8,128)(2,1)}) %all-gather.3.cloned.1.call-update) | async-done | bytes 6963216 | tf_op jit(solution)/shard_map/all_gather | solution.py:94
  128.3 4.6 %fusion.2 = f32[1088]{0:T(1024)S(1)} fusion(bf16[1,1088,3200]{2,1,0:T(8,128)(2,1)} %all-gather.3.cloned.1.call-done), kind=kLoop, calls=%fused_computation.7 | loop fusion | flops 10443712 | bytes 6967552 | tf_op jit(solution)/shard_map/reduce_sum | solution.py:99
  132.9 0.4 copy-done
  133.3 9.5 %fusion.6 = f32[1088,768]{0,1:T(8,128)S(1)} fusion(bf16[3200,768]{1,0:T(8,128)(2,1)} %pad_maximum_fusion, bf16[1,1088,3200]{2,1,0:T(8,128)(2,1)S(1)} %copy-done, f32[3200]{0:T(1024)S(1)} %copy-done.8, f32[1088]{0:T(1024)S(1)} %add_rsqrt_fusion), kind=kOutput, calls=%fused_computation.12 | convolution fusion | flops 5361664000 | bytes 15237888 | tf_op jit(solution)/shard_map/dot_general | solution.py:101
  143.1 0.6 broadcast_in_dim.96
  143.8 5.6 %all-to-all-start.3 = ((f32[8,2,1088]{2,1,0:T(2,128)}), f32[8,2,1088]{2,1,0:T(2,128)}, u32[]{:S(2)}, u32[]{:S(2)}) async-start(f32[8,2,1088]{2,1,0:T(2,128)} %broadcast_in_dim.96), calls=%async_computation.3 | async-start | bytes 147456 | tf_op jit(solution)/shard_map/all_to_all | solution.py:49
  149.4 0.9 fusion.21
  150.3 5.9 %all-to-all-done.3 = f32[8,2,1088]{2,1,0:T(2,128)} async-done(((f32[8,2,1088]{2,1,0:T(2,128)}), f32[8,2,1088]{2,1,0:T(2,128)}, u32[]{:S(2)}, u32[]{:S(2)}) %all-to-all-start.3) | async-done | bytes 69664 | tf_op jit(solution)/shard_map/all_to_all | solution.py:49
  156.1 0.9 reduce_sum.57
  157.1 0.9 fusion.17
  158.1 0.3 pad_maximum_fusion.1
  158.6 0.9 copy.116
  159.4 0.3 collective-permute-start.3
  159.7 0.9 copy.115
  160.6 1.4 collective-permute-done.3
  162.9 3.2 fusion.45
  166.2 4.9 %fusion.12 = bf16[2,1025,128]{2,1,0:T(8,128)(2,1)S(1)} fusion(bf16[2,1025,128]{2,1,0:T(8,128)(2,1)S(1)} %reshape_squeeze.11, f32[2,1025]{1,0:T(2,128)S(1)} %fusion.45, bf16[2,1025,128]{2,1,0:T(8,128)(2,1)S(1)} %reshape_squeeze.9, bf16[2,1025,128]{2,1,0:T(8,128)(2,1)S(1)} %reshape_squeeze.10), kind=kOutput, calls=%fused_computation.19 | convolution fusion | flops 1084510464 | bytes 2107400 | tf_op jit(solution)/shard_map/sqk,skc->sqc/dot_general | solution.py:140
  171.2 3.0 broadcast_in_dim.98
  174.3 5.7 %all-to-all-start.4 = ((bf16[16,1088,128]{2,1,0:T(8,128)(2,1)}), bf16[16,1088,128]{2,1,0:T(8,128)(2,1)}, u32[]{:S(2)}, u32[]{:S(2)}) async-start(bf16[16,1088,128]{2,1,0:T(8,128)(2,1)} %bitcast.100), calls=%async_computation.4 | async-start | bytes 8912896 | tf_op jit(solution)/shard_map/all_to_all | solution.py:153
  180.0 0.9 dynamic_slice.41
  181.1 1.9 constant_dynamic-slice_fusion.3
  182.9 1.6 copy.130
  184.5 55.5 %all-to-all-done.4 = bf16[16,1088,128]{2,1,0:T(8,128)(2,1)} async-done(((bf16[16,1088,128]{2,1,0:T(8,128)(2,1)}), bf16[16,1088,128]{2,1,0:T(8,128)(2,1)}, u32[]{:S(2)}, u32[]{:S(2)}) %all-to-all-start.4) | async-done | bytes 4456480 | tf_op jit(solution)/shard_map/all_to_all | solution.py:153
  240.0 11.4 %convolution_convert_fusion = bf16[16,1088,400]{1,2,0:T(8,128)(2,1)} fusion(bf16[16,1088,128]{2,1,0:T(8,128)(2,1)} %all-to-all-done.4, bf16[2048,400]{0,1:T(8,128)(2,1)S(1)} %copy-done.1), kind=kOutput, calls=%fused_computation.2 | convolution fusion | flops 1789542400 | bytes 20021248 | tf_op jit(solution)/shard_map/hsc,hcd->hsd/dot_general | solution.py:160
  251.4 7.8 %convert_reduce_fusion = f32[1088,400]{0,1:T(8,128)S(1)} fusion(bf16[16,1088,400]{1,2,0:T(8,128)(2,1)} %convolution_convert_fusion), kind=kLoop, calls=%fused_computation.1 | loop fusion | flops 13491200 | bytes 15667200 | tf_op jit(solution)/shard_map/reduce_sum | solution.py:166
  259.2 0.3 fusion.13
  259.6 0.3 collective-permute-start.4
  260.0 1.8 collective-permute-done.4
  262.0 0.2 copy.121
  262.8 0.2 fusion.43
  263.0 1.0 reshape.275
  264.1 1.0 reshape.276
  265.1 4.9 %copy.125 = bf16[16,16,200,2,2]{1,0,4,3,2:T(8,128)(2,1)S(1)} copy(bf16[16,16,200,2,2]{2,4,1,3,0:T(2,128)(2,1)} %bitcast.115) | data formatting | bytes 819200 | tf_op jit(solution)/shard_map/transpose | solution.py:20
  270.0 3.9 stack_reshape.23
  273.8 4.9 %copy.124 = bf16[16,16,200,2,2]{1,0,4,3,2:T(8,128)(2,1)S(1)} copy(bf16[16,16,200,2,2]{2,4,1,3,0:T(2,128)(2,1)} %bitcast.114) | data formatting | bytes 819200 | tf_op jit(solution)/shard_map/transpose | solution.py:20
  278.7 3.8 stack_reshape.22
  282.6 1.2 pad_maximum_fusion.7
  283.8 3.3 broadcast_select_fusion
  287.1 4.8 %all-to-all-start.5 = ((bf16[8,2,256,800]{2,3,1,0:T(8,128)(2,1)}), bf16[8,2,256,800]{2,3,1,0:T(8,128)(2,1)}, u32[]{:S(2)}, u32[]{:S(2)}) async-start(bf16[8,2,256,800]{2,3,1,0:T(8,128)(2,1)} %broadcast_select_fusion), calls=%async_computation.5 | async-start | bytes 13107200 | tf_op jit(solution)/shard_map/all_to_all | solution.py:183
  292.1 0.6 select_reduce_fusion.3
  294.1 0.7 fusion.39
  294.8 0.7 select_reduce_fusion.2
  296.8 0.7 select_reduce_fusion
  302.7 80.9 %all-to-all-done.5 = bf16[8,2,256,800]{2,3,1,0:T(8,128)(2,1)} async-done(((bf16[8,2,256,800]{2,3,1,0:T(8,128)(2,1)}), bf16[8,2,256,800]{2,3,1,0:T(8,128)(2,1)}, u32[]{:S(2)}, u32[]{:S(2)}) %all-to-all-start.5) | async-done | bytes 6553632 | tf_op jit(solution)/shard_map/all_to_all | solution.py:183
  383.6 4.0 %dynamic-slice_select_fusion.3 = (bf16[1,256,800]{1,2,0:T(8,128)(2,1)S(1)}, bf16[1,256,800]{1,2,0:T(8,128)(2,1)S(1)}, bf16[1,256,800]{1,2,0:T(8,128)(2,1)S(1)}, bf16[1,256,800]{1,2,0:T(8,128)(2,1)S(1)}) fusion(bf16[16,256,800]{1,2,0:T(8,128)(2,1)} %bitcast.30, s32[]{:T(128)S(6)} %select_n.180, pred[]{:T(512)} %get-tuple-element.44, s32[]{:T(128)S(6)} %select_n.192, ...), kind=kLoop, calls=%fused_computation.54 | loop fusion | flops 819200 | bytes 3276820 | tf_op jit(solution)/shard_map/jit(_where)/select_n | solution.py:43
  387.6 1.4 pad_maximum_fusion.4
  (60 shorter events, 3.2 us)
Async XLA Ops:
  6.5 20.7 %copy-start.4 = (bf16[400,384]{1,0:T(8,128)(2,1)S(1)}, bf16[400,384]{1,0:T(8,128)(2,1)}, u32[]{:S(2)}) copy-start(bf16[400,384]{1,0:T(8,128)(2,1)} %param.10) | copy-start | bytes 921604
  6.5 121.8 %all-gather.3.cloned.1.call-start = ((), (), s32[]{:S(2)}) async-start(), calls=%async_computation.6 | async-start | bytes 7833600 | tf_op jit(solution)/shard_map/all_gather | solution.py:94
  29.0 38.1 %all-to-all-start = ((bf16[8,400,384]{2,1,0:T(8,128)(2,1)}), bf16[8,400,384]{2,1,0:T(8,128)(2,1)S(1)}, u32[]{:S(2)}, u32[]{:S(2)}) async-start(bf16[8,400,384]{2,1,0:T(8,128)(2,1)} %broadcast_in_dim.94), calls=%async_computation | async-start | bytes 4915200 | tf_op jit(solution)/shard_map/all_to_all | solution.py:55
  34.1 57.7 %copy-start.7 = (f32[2,128]{1,0:T(2,128)S(1)}, f32[2,128]{1,0:T(2,128)}, u32[]{:S(2)}) copy-start(f32[2,128]{1,0:T(2,128)} %param.11) | copy-start | bytes 3076
  67.1 23.1 %all-to-all-start.2 = ((bf16[16,128,200]{1,2,0:T(8,128)(2,1)}), bf16[16,128,200]{1,2,0:T(8,128)(2,1)S(1)}, u32[]{:S(2)}, u32[]{:S(2)}) async-start(bf16[16,128,200]{1,2,0:T(8,128)(2,1)} %copy.108), calls=%async_computation.2 | async-start | bytes 1638400 | tf_op jit(solution)/shard_map/all_to_all | solution.py:82
  75.1 22.3 %collective-permute-start = (bf16[3200,384]{1,0:T(8,128)(2,1)S(1)}, bf16[3200,384]{1,0:T(8,128)(2,1)}, u32[]{:S(2)}, u32[]{:S(2)}) collective-permute-start(bf16[3200,384]{1,0:T(8,128)(2,1)S(1)} %bitcast.101), channel_id=1, source_target_pairs={{0,1},{1,0},{2,3},{3,2},{4,5},{5,4},{6,7},{7,6},{8,9},{9,8},{10,11... | collective-permute-start | bytes 7372808 | tf_op jit(solution)/shard_map/ppermute | solution.py:60
  91.1 3.5 collective-permute-start.1
  91.8 2.3 collective-permute-start.2
  128.3 5.0 %copy-start = (bf16[1,1088,3200]{2,1,0:T(8,128)(2,1)S(1)}, bf16[1,1088,3200]{2,1,0:T(8,128)(2,1)}, u32[]{:S(2)}) copy-start(bf16[1,1088,3200]{2,1,0:T(8,128)(2,1)} %all-gather.3.cloned.1.call-done) | copy-start | bytes 20889604
  128.3 5.0 %copy-start.8 = (f32[3200]{0:T(1024)S(1)}, f32[3200]{0:T(1024)}, u32[]{:S(2)}) copy-start(f32[3200]{0:T(1024)} %param.9) | copy-start | bytes 38404
  143.8 12.4 %all-to-all-start.3 = ((f32[8,2,1088]{2,1,0:T(2,128)}), f32[8,2,1088]{2,1,0:T(2,128)}, u32[]{:S(2)}, u32[]{:S(2)}) async-start(f32[8,2,1088]{2,1,0:T(2,128)} %broadcast_in_dim.96), calls=%async_computation.3 | async-start | bytes 147456 | tf_op jit(solution)/shard_map/all_to_all | solution.py:49
  157.1 1.1 copy-start.3
  159.4 2.6 collective-permute-start.3
  174.3 6.6 %copy-start.5 = (s32[8,2]{0,1:T(2,128)S(1)}, s32[8,2]{0,1:T(2,128)}, u32[]{:S(2)}) copy-start(s32[8,2]{0,1:T(2,128)} %param.14) | copy-start | bytes 196
  174.3 6.6 %copy-start.6 = (s32[8,2]{0,1:T(2,128)S(1)}, s32[8,2]{0,1:T(2,128)}, u32[]{:S(2)}) copy-start(s32[8,2]{0,1:T(2,128)} %param.15) | copy-start | bytes 196
  174.3 65.7 %all-to-all-start.4 = ((bf16[16,1088,128]{2,1,0:T(8,128)(2,1)}), bf16[16,1088,128]{2,1,0:T(8,128)(2,1)}, u32[]{:S(2)}, u32[]{:S(2)}) async-start(bf16[16,1088,128]{2,1,0:T(8,128)(2,1)} %bitcast.100), calls=%async_computation.4 | async-start | bytes 8912896 | tf_op jit(solution)/shard_map/all_to_all | solution.py:153
  180.0 60.0 %copy-start.1 = (bf16[2048,400]{0,1:T(8,128)(2,1)S(1)}, bf16[2048,400]{0,1:T(8,128)(2,1)}, u32[]{:S(2)}) copy-start(bf16[2048,400]{0,1:T(8,128)(2,1)} %pad_maximum_fusion.3) | copy-start | bytes 4915204
  251.4 7.8 %copy-start.2 = (bf16[1,1088,400]{1,2,0:T(8,128)(2,1)S(1)}, bf16[1,1088,400]{1,2,0:T(8,128)(2,1)}, u32[]{:S(2)}) copy-start(bf16[1,1088,400]{1,2,0:T(8,128)(2,1)} %copy.130) | copy-start | bytes 2611204
  259.6 2.2 collective-permute-start.4
  287.1 96.5 %all-to-all-start.5 = ((bf16[8,2,256,800]{2,3,1,0:T(8,128)(2,1)}), bf16[8,2,256,800]{2,3,1,0:T(8,128)(2,1)}, u32[]{:S(2)}, u32[]{:S(2)}) async-start(bf16[8,2,256,800]{2,3,1,0:T(8,128)(2,1)} %broadcast_select_fusion), calls=%async_computation.5 | async-start | bytes 13107200 | tf_op jit(solution)/shard_map/all_to_all | solution.py:183
Sparse Core Ops, SparseCore 0:
  9.7 118.6 all-gather.2
where the time goes:
time: 397 us; the launch traced here: 396 us
  waiting for transfers between devices  220 us (55%)
  local copies, waits for them, and re-layouts  39.9 us (10%)
  other arithmetic  36.9 us (9%)
  starting transfers between devices  29.1 us (7%)
  matrix products  29 us (7%)
  between operations  21.5 us (5%)
  blocking collectives  19 us (5%)
    all_to_all x1, waiting for transfers between devices, body(): lax.all_to_all(outgoing, 'fsdp', split_axis=0, concat_axis=0, tiled=True)  80.9 us
    all_to_all x1, waiting for transfers between devices, body(): lax.all_to_all(outgoing.reshape(groups, half_length, HEAD_DIM), ('chip',...  55.5 us
    all_to_all x1, waiting for transfers between devices, gather_blocks(): lax.all_to_all(spread, axis_name, split_axis=0, concat_axis=0, tiled=True)  30.7 us
    all_gather x1, waiting for transfers between devices, body(): half = lax.all_gather(own_rows, 'chip', axis=0, tiled=True)  26.1 us
    all_to_all x1, blocking collectives, body(): lax.all_to_all(spread, 'fsdp', split_axis=0, concat_axis=0, tiled=True)  19 us
    all_to_all x1, waiting for transfers between devices, body(): lax.all_to_all(head_rows.reshape(groups, HEAD_DIM, block), ('chip', 'core...  15 us
    dot_general x1, matrix products, body(): jnp.einsum('hsc,hcd->hsd', all_heads, pair_weight.reshape(groups, HEAD_DI...  11.4 us
    transpose x2, local copies, waits for them, and re-layouts, merge_tiles(): patches.reshape(halves, 2, halves, 2, columns).transpose(0, 2, 4, 1, 3)  9.74 us
  transfers between devices with their start and end apart: 11, of which 9 were waited for; matrix products, arithmetic and copies ran while one was open for 6% of the time, Pallas kernels for 0%

commit v1 on v0

--- a/solution.py
+++ b/solution.py
@@ -91,7 +91,9 @@
     pair_qkv = pair_up(full_qkv, core, swap, 1)
     pair_qkv, pair_weight = lax.optimization_barrier((pair_qkv, pair_weight))
     pair_gain = pair_up(qk_gain, core, swap, 1).reshape(2, cores, HEAD_DIM)
-    half = lax.all_gather(own_rows, "chip", axis=0, tiled=True)
+    half = jnp.concatenate(
+        lax.all_to_all(jnp.stack([own_rows] * lax.axis_size("chip")), "chip", 0, 0), axis=0
+    )
     half_length = half.shape[0]
     piece = own_rows.shape[0]
     values = half.astype(jnp.float32)

time: 397 us -> 455 us (1.15)
  blocking collectives: 19 us -> 74 us
  between operations: 21.5 us -> 8.41 us
  waiting for transfers between devices: 220 us -> 228 us
  local copies, waits for them, and re-layouts: 39.9 us -> 44.5 us
    all_to_all x0 -> x2, blocking collectives: none -> 55.1 us  [the longest x1 34.6 us: gather_blocks(): lax.all_to_all(spread, axis_name, split_axis=0, concat_axis=0, tiled=True)]
    all_to_all x2 -> x1, waiting for transfers between devices: 45.7 us -> 77.2 us  [body(): lax.all_to_all(jnp.stack([own_rows] * lax.axis_size('chip')), 'chip', 0, 0)]
    all_gather x1 -> x0, waiting for transfers between devices: 26.1 us -> none  [body(): half = lax.all_gather(own_rows, 'chip', axis=0, tiled=True)]
    dot_general x0 -> x1, local copies, waits for them, and re-layouts: none -> 7.43 us  [body(): projected = jnp.dot(normed, pair_qkv, preferred_element_type=jnp.float32)]
    convert_element_type x0 -> x1, other arithmetic: none -> 5.67 us  [body(): normed = (values * lax.rsqrt(jnp.mean(values * values, axis=-1, keepdims=...]
    all_to_all x2 -> x1, starting transfers between devices: 11.6 us -> 6.64 us  [body(): lax.all_to_all(jnp.stack([own_rows] * lax.axis_size('chip')), 'chip', 0, 0)]
  transfers between devices with their start and end apart: 11 -> 9, of which waited for: 9 -> 7; matrix products, arithmetic and copies ran while one was open for 6% -> 5% of each run, Pallas kernels for 0% -> 0%
where the time goes in v1:
time: 455 us; the launch traced here: 450 us
  waiting for transfers between devices  228 us (50%)
  blocking collectives  74 us (16%)
  local copies, waits for them, and re-layouts  44.5 us (10%)
  other arithmetic  40.5 us (9%)
  starting transfers between devices  27.8 us (6%)
  matrix products  27.7 us (6%)
  between operations  8.41 us (2%)
    all_to_all x1, waiting for transfers between devices, body(): lax.all_to_all(outgoing, 'fsdp', split_axis=0, concat_axis=0, tiled=True)  80.9 us
    all_to_all x1, waiting for transfers between devices, body(): lax.all_to_all(jnp.stack([own_rows] * lax.axis_size('chip')), 'chip', 0, 0)  77.2 us
    all_to_all x1, waiting for transfers between devices, body(): lax.all_to_all(outgoing.reshape(groups, half_length, HEAD_DIM), ('chip',...  55.5 us
    all_to_all x1, blocking collectives, gather_blocks(): lax.all_to_all(spread, axis_name, split_axis=0, concat_axis=0, tiled=True)  34.6 us
    all_to_all x1, blocking collectives, body(): lax.all_to_all(head_rows.reshape(groups, HEAD_DIM, block), ('chip', 'core...  20.4 us
    all_to_all x1, blocking collectives, body(): lax.all_to_all(spread, 'fsdp', split_axis=0, concat_axis=0, tiled=True)  18.9 us
    dot_general x1, matrix products, body(): jnp.einsum('hsc,hcd->hsd', all_heads, pair_weight.reshape(groups, HEAD_DI...  11.4 us
    transpose x2, local copies, waits for them, and re-layouts, merge_tiles(): patches.reshape(halves, 2, halves, 2, columns).transpose(0, 2, 4, 1, 3)  9.74 us
  transfers between devices with their start and end apart: 9, of which 7 were waited for; matrix products, arithmetic and copies ran while one was open for 5% of the time, Pallas kernels for 0%

profile of v1, /device:TPU:8, one launch (start us, length us, event | category | flops | bytes accessed | tf_op | source)
XLA Modules:
  0.0 450.5 jit_solution(17022489450399082636)
XLA Ops:
  0.0 1.0 broadcast_in_dim.95
  1.0 18.9 %all_to_all.35 = bf16[8,128,400]{1,2,0:T(8,128)(2,1)S(1)} all-to-all(bf16[8,128,400]{1,2,0:T(8,128)(2,1)S(1)} %broadcast_in_dim.95), channel_id=1, replica_groups=mesh['fsdp'=8,'chip'=8,'core'=2] {'fsdp'}, dimensions={0} | all-to-all | bytes 1638400 | tf_op jit(solution)/shard_map/all_to_all | solution.py:79
  20.2 0.3 reshape.284
  20.5 0.2 copy.81
  20.7 20.4 %all_to_all.36 = bf16[16,128,200]{1,2,0:T(8,128)(2,1)S(1)} all-to-all(bf16[16,128,200]{1,2,0:T(8,128)(2,1)S(1)} %copy.81), channel_id=1, replica_groups=mesh['fsdp'=8,'chip'=8,'core'=2] {'chip','core'}, dimensions={0} | all-to-all | bytes 1638400 | tf_op jit(solution)/shard_map/all_to_all | solution.py:82
  41.2 0.2 broadcast_in_dim.94
  41.4 34.6 %all_to_all.37 = bf16[8,400,384]{2,1,0:T(8,128)(2,1)S(1)} all-to-all(bf16[8,400,384]{2,1,0:T(8,128)(2,1)S(1)} %broadcast_in_dim.94), channel_id=1, replica_groups=mesh['fsdp'=8,'chip'=8,'core'=2] {'fsdp'}, dimensions={0} | all-to-all | bytes 4915200 | tf_op jit(solution)/shard_map/all_to_all | solution.py:55
  76.0 3.4 stack.34
  79.4 6.6 %all-to-all-start = ((bf16[8,136,3200]{2,1,0:T(8,128)(2,1)}), bf16[8,136,3200]{2,1,0:T(8,128)(2,1)}, u32[]{:S(2)}, u32[]{:S(2)}) async-start(bf16[8,136,3200]{2,1,0:T(8,128)(2,1)} %stack.34), calls=%async_computation | async-start | bytes 13926400 | tf_op jit(solution)/shard_map/all_to_all | solution.py:95
  86.1 1.0 copy_bitcast_fusion
  87.1 0.5 collective-permute-start.1
  87.6 0.3 collective-permute-start.2
  87.9 4.2 collective-permute-done.2
  92.1 1.5 broadcast_select_fusion.4
  93.6 1.3 pad_maximum_fusion.3
  94.8 2.1 broadcast_select_fusion.2
  97.0 2.6 pad_maximum_fusion
  99.6 7.4 %copy.83 = bf16[768,3200]{1,0:T(8,128)(2,1)} copy(bf16[768,3200]{0,1:T(8,128)(2,1)} %bitcast.105) | data formatting | bytes 9830400 | tf_op jit(solution)/shard_map/dot_general | solution.py:103
  107.0 77.2 %all-to-all-done = bf16[8,136,3200]{2,1,0:T(8,128)(2,1)} async-done(((bf16[8,136,3200]{2,1,0:T(8,128)(2,1)}), bf16[8,136,3200]{2,1,0:T(8,128)(2,1)}, u32[]{:S(2)}, u32[]{:S(2)}) %all-to-all-start) | async-done | bytes 6963232 | tf_op jit(solution)/shard_map/all_to_all | solution.py:95
  184.2 4.4 fusion.2
  188.7 5.7 %fusion.4 = bf16[8,136,3200]{2,1,0:T(8,128)(2,1)S(1)} fusion(bf16[8,136,3200]{2,1,0:T(8,128)(2,1)} %all-to-all-done, f32[3200]{0:T(1024)S(1)} %copy-done.5, f32[8,136]{1,0:T(8,128)S(1)} %add_rsqrt_fusion), kind=kLoop, calls=%fused_computation.9 | loop fusion | flops 13926400 | bytes 13943552 | tf_op jit(solution)/shard_map/convert_element_type | solution.py:102
  194.3 8.2 %fusion.41 = f32[1088,2,3,128]{3,0,2,1:T(8,128)S(1)} fusion(bf16[1088,3200,1,1]{1,0,3,2:T(8,128)(2,1)S(1)} %bitcast.108, bf16[2,3,128,3200]{3,2,1,0:T(8,128)(2,1)} %bitcast.110), kind=kOutput, calls=%fused_computation.105 | convolution fusion | flops 5347737600 | bytes 15220736 | tf_op jit(solution)/shard_map/dot_general | solution.py:103
  202.6 0.4 fusion.15
  203.0 0.6 broadcast_in_dim.96
  203.7 8.7 %all-to-all-start.4 = ((f32[8,2,1088]{2,1,0:T(2,128)}), f32[8,2,1088]{2,1,0:T(2,128)S(1)}, u32[]{:S(2)}, u32[]{:S(2)}) async-start(f32[8,2,1088]{2,1,0:T(2,128)} %broadcast_in_dim.96), calls=%async_computation.4 | async-start | bytes 147456 | tf_op jit(solution)/shard_map/all_to_all | solution.py:49
  212.3 0.9 fusion.16
  213.2 5.7 %all-to-all-done.4 = f32[8,2,1088]{2,1,0:T(2,128)S(1)} async-done(((f32[8,2,1088]{2,1,0:T(2,128)}), f32[8,2,1088]{2,1,0:T(2,128)S(1)}, u32[]{:S(2)}, u32[]{:S(2)}) %all-to-all-start.4) | async-done | bytes 69664 | tf_op jit(solution)/shard_map/all_to_all | solution.py:49
  219.0 0.4 fusion.13
  219.4 0.6 copy-done.2
  220.3 0.6 collective-permute-start.3
  220.9 2.3 collective-permute-done.3
  224.0 3.2 fusion.40
  227.2 4.9 %fusion.7 = bf16[2,1025,128]{2,1,0:T(8,128)(2,1)S(1)} fusion(bf16[2,1025,128]{2,1,0:T(8,128)(2,1)S(1)} %reshape_squeeze.11, f32[2,1025]{1,0:T(2,128)S(1)} %fusion.40, bf16[2,1025,128]{2,1,0:T(8,128)(2,1)S(1)} %reshape_squeeze.9, bf16[2,1025,128]{2,1,0:T(8,128)(2,1)S(1)} %reshape_squeeze.10), kind=kOutput, calls=%fused_computation.15 | convolution fusion | flops 1084510464 | bytes 2107400 | tf_op jit(solution)/shard_map/sqk,skc->sqc/dot_general | solution.py:142
  232.3 3.0 broadcast_in_dim.98
  235.3 6.0 %all-to-all-start.5 = ((bf16[16,1088,128]{2,1,0:T(8,128)(2,1)}), bf16[16,1088,128]{2,1,0:T(8,128)(2,1)}, u32[]{:S(2)}, u32[]{:S(2)}) async-start(bf16[16,1088,128]{2,1,0:T(8,128)(2,1)} %bitcast.106), calls=%async_computation.5 | async-start | bytes 8912896 | tf_op jit(solution)/shard_map/all_to_all | solution.py:155
  241.4 0.9 dynamic_slice.41
  242.4 1.9 constant_dynamic-slice_fusion.1
  244.3 1.6 copy.98
  245.9 55.5 %all-to-all-done.5 = bf16[16,1088,128]{2,1,0:T(8,128)(2,1)} async-done(((bf16[16,1088,128]{2,1,0:T(8,128)(2,1)}), bf16[16,1088,128]{2,1,0:T(8,128)(2,1)}, u32[]{:S(2)}, u32[]{:S(2)}) %all-to-all-start.5) | async-done | bytes 4456480 | tf_op jit(solution)/shard_map/all_to_all | solution.py:155
  301.4 11.4 %convolution_convert_fusion = bf16[16,1088,400]{1,2,0:T(8,128)(2,1)} fusion(bf16[16,1088,128]{2,1,0:T(8,128)(2,1)} %all-to-all-done.5, bf16[2048,400]{0,1:T(8,128)(2,1)S(1)} %copy-done), kind=kOutput, calls=%fused_computation.2 | convolution fusion | flops 1789542400 | bytes 20021248 | tf_op jit(solution)/shard_map/hsc,hcd->hsd/dot_general | solution.py:162
  312.8 7.8 %convert_reduce_fusion = f32[1088,400]{0,1:T(8,128)S(1)} fusion(bf16[16,1088,400]{1,2,0:T(8,128)(2,1)} %convolution_convert_fusion), kind=kLoop, calls=%fused_computation.1 | loop fusion | flops 13491200 | bytes 15667200 | tf_op jit(solution)/shard_map/reduce_sum | solution.py:168
  320.6 0.3 add_convert_fusion
  321.0 0.3 collective-permute-start.4
  321.3 1.8 collective-permute-done.4
  323.3 0.2 copy.90
  323.5 0.2 copy.91
  323.8 0.2 pad_maximum_fusion.5
  324.1 0.2 fusion.38
  324.3 1.0 reshape.292
  325.4 1.0 reshape.293
  326.4 4.9 %copy.94 = bf16[16,16,200,2,2]{1,0,4,3,2:T(8,128)(2,1)S(1)} copy(bf16[16,16,200,2,2]{2,4,1,3,0:T(2,128)(2,1)} %bitcast.119) | data formatting | bytes 819200 | tf_op jit(solution)/shard_map/transpose | solution.py:20
  331.3 3.9 stack_reshape.23
  335.1 4.9 %copy.93 = bf16[16,16,200,2,2]{1,0,4,3,2:T(8,128)(2,1)S(1)} copy(bf16[16,16,200,2,2]{2,4,1,3,0:T(2,128)(2,1)} %bitcast.118) | data formatting | bytes 819200 | tf_op jit(solution)/shard_map/transpose | solution.py:20
  340.0 3.8 stack_reshape.22
  343.9 1.2 pad_maximum_fusion.7
  345.1 3.3 broadcast_select_fusion
  348.4 4.8 %all-to-all-start.6 = ((bf16[8,2,256,800]{2,3,1,0:T(8,128)(2,1)}), bf16[8,2,256,800]{2,3,1,0:T(8,128)(2,1)}, u32[]{:S(2)}, u32[]{:S(2)}) async-start(bf16[8,2,256,800]{2,3,1,0:T(8,128)(2,1)} %broadcast_select_fusion), calls=%async_computation.6 | async-start | bytes 13107200 | tf_op jit(solution)/shard_map/all_to_all | solution.py:185
  353.5 0.6 select_reduce_fusion.3
  355.4 0.7 fusion.34
  356.1 0.7 select_reduce_fusion.2
  358.1 0.7 select_reduce_fusion
  364.0 80.9 %all-to-all-done.6 = bf16[8,2,256,800]{2,3,1,0:T(8,128)(2,1)} async-done(((bf16[8,2,256,800]{2,3,1,0:T(8,128)(2,1)}), bf16[8,2,256,800]{2,3,1,0:T(8,128)(2,1)}, u32[]{:S(2)}, u32[]{:S(2)}) %all-to-all-start.6) | async-done | bytes 6553632 | tf_op jit(solution)/shard_map/all_to_all | solution.py:185
  444.9 4.0 dynamic-slice_select_fusion.3
  448.9 1.4 pad_maximum_fusion.4
  (56 shorter events, 2.4 us)
Async XLA Ops:
  20.5 20.7 %copy-start.4 = (bf16[400,384]{1,0:T(8,128)(2,1)S(1)}, bf16[400,384]{1,0:T(8,128)(2,1)}, u32[]{:S(2)}) copy-start(bf16[400,384]{1,0:T(8,128)(2,1)} %param.10) | copy-start | bytes 921604
  41.4 34.6 %copy-start.3 = (bf16[1,136,3200]{2,1,0:T(8,128)(2,1)S(1)}, bf16[1,136,3200]{2,1,0:T(8,128)(2,1)}, u32[]{:S(2)}) copy-start(bf16[1,136,3200]{2,1,0:T(8,128)(2,1)} %param.8) | copy-start | bytes 2611204
  79.4 8.1 %copy-start.8 = (f32[2,128]{1,0:T(2,128)S(1)}, f32[2,128]{1,0:T(2,128)}, u32[]{:S(2)}) copy-start(f32[2,128]{1,0:T(2,128)} %param.11) | copy-start | bytes 3076
  79.4 104.8 %all-to-all-start = ((bf16[8,136,3200]{2,1,0:T(8,128)(2,1)}), bf16[8,136,3200]{2,1,0:T(8,128)(2,1)}, u32[]{:S(2)}, u32[]{:S(2)}) async-start(bf16[8,136,3200]{2,1,0:T(8,128)(2,1)} %stack.34), calls=%async_computation | async-start | bytes 13926400 | tf_op jit(solution)/shard_map/all_to_all | solution.py:95
  86.1 8.8 %collective-permute-start = (bf16[3200,384]{1,0:T(8,128)(2,1)S(1)}, bf16[3200,384]{1,0:T(8,128)(2,1)}, u32[]{:S(2)}, u32[]{:S(2)}) collective-permute-start(bf16[3200,384]{1,0:T(8,128)(2,1)S(1)} %bitcast.107), channel_id=1, source_target_pairs={{0,1},{1,0},{2,3},{3,2},{4,5},{5,4},{6,7},{7,6},{8,9},{9,8},{10,11... | collective-permute-start | bytes 7372808 | tf_op jit(solution)/shard_map/ppermute | solution.py:60
  87.1 5.0 %collective-permute-start.1 = (bf16[2048,200]{0,1:T(8,128)(2,1)}, bf16[2048,200]{0,1:T(8,128)(2,1)}, u32[]{:S(2)}, u32[]{:S(2)}) collective-permute-start(bf16[2048,200]{0,1:T(8,128)(2,1)} %copy_bitcast_fusion), channel_id=1, source_target_pairs={{0,1},{1,0},{2,3},{3,2},{4,5},{5,4},{6,7},{7,6},{8,9},{9,8},{10,11... | collective-permute-start | bytes 2457608 | tf_op jit(solution)/shard_map/ppermute | solution.py:60
  87.6 4.5 collective-permute-start.2
  107.0 81.6 %copy-start.5 = (f32[3200]{0:T(1024)S(1)}, f32[3200]{0:T(1024)}, u32[]{:S(2)}) copy-start(f32[3200]{0:T(1024)} %param.9) | copy-start | bytes 38404
  203.7 15.3 %all-to-all-start.4 = ((f32[8,2,1088]{2,1,0:T(2,128)}), f32[8,2,1088]{2,1,0:T(2,128)S(1)}, u32[]{:S(2)}, u32[]{:S(2)}) async-start(f32[8,2,1088]{2,1,0:T(2,128)} %broadcast_in_dim.96), calls=%async_computation.4 | async-start | bytes 147456 | tf_op jit(solution)/shard_map/all_to_all | solution.py:49
  219.0 1.1 copy-start.2
  220.3 3.0 collective-permute-start.3
  235.3 7.0 %copy-start.6 = (s32[8,2]{0,1:T(2,128)S(1)}, s32[8,2]{0,1:T(2,128)}, u32[]{:S(2)}) copy-start(s32[8,2]{0,1:T(2,128)} %param.14) | copy-start | bytes 196
  235.3 7.0 %copy-start.7 = (s32[8,2]{0,1:T(2,128)S(1)}, s32[8,2]{0,1:T(2,128)}, u32[]{:S(2)}) copy-start(s32[8,2]{0,1:T(2,128)} %param.15) | copy-start | bytes 196
  235.3 66.1 %all-to-all-start.5 = ((bf16[16,1088,128]{2,1,0:T(8,128)(2,1)}), bf16[16,1088,128]{2,1,0:T(8,128)(2,1)}, u32[]{:S(2)}, u32[]{:S(2)}) async-start(bf16[16,1088,128]{2,1,0:T(8,128)(2,1)} %bitcast.106), calls=%async_computation.5 | async-start | bytes 8912896 | tf_op jit(solution)/shard_map/all_to_all | solution.py:155
  241.3 60.0 %copy-start = (bf16[2048,400]{0,1:T(8,128)(2,1)S(1)}, bf16[2048,400]{0,1:T(8,128)(2,1)}, u32[]{:S(2)}) copy-start(bf16[2048,400]{0,1:T(8,128)(2,1)} %pad_maximum_fusion.3) | copy-start | bytes 4915204
  312.8 7.8 %copy-start.1 = (bf16[1088,400]{0,1:T(8,128)(2,1)S(1)}, bf16[1088,400]{0,1:T(8,128)(2,1)}, u32[]{:S(2)}) copy-start(bf16[1088,400]{0,1:T(8,128)(2,1)} %copy.98) | copy-start | bytes 2611204
  321.0 2.1 collective-permute-start.4
  348.4 96.5 %all-to-all-start.6 = ((bf16[8,2,256,800]{2,3,1,0:T(8,128)(2,1)}), bf16[8,2,256,800]{2,3,1,0:T(8,128)(2,1)}, u32[]{:S(2)}, u32[]{:S(2)}) async-start(bf16[8,2,256,800]{2,3,1,0:T(8,128)(2,1)} %broadcast_select_fusion), calls=%async_computation.6 | async-start | bytes 13107200 | tf_op jit(solution)/shard_map/all_to_all | solution.py:185
